TPU v7x, 256 devices: a whole 4x4x8 slice. The times are simulated.
256 devices in a mesh: req: 64 (over z, y, core), tp: 4 (over x).
Axes of the slice: x: 4, y: 4, z: 8, core: 2. Of those that a mesh axis runs over, the one named last changes fastest.
Arguments:
- hidden_in: bfloat16 [8192, 2048], P('req'), may hold values from -6 to 6
- attn_gain: float32 [2048], replicated, may hold values from 0.1 to 1.9
- w_query: bfloat16 [2048, 3072], P(None, 'tp'), may hold values from -0.125 to 0.125
- w_latent: bfloat16 [2048, 576], P(None, 'tp'), may hold values from -0.125 to 0.125
- kv_gain: float32 [512], replicated, may hold values from 0.1 to 1.9
- w_key_up: bfloat16 [512, 2048], P(None, 'tp'), may hold values from -0.25 to 0.25
- w_value_up: bfloat16 [512, 2048], P(None, 'tp'), may hold values from -0.25 to 0.25
- w_out: bfloat16 [2048, 2048], P('tp'), may hold values from -0.125 to 0.125
- moe_gain: float32 [2048], replicated, may hold values from 0.1 to 1.9
- w_gate: bfloat16 [64, 2048, 1408], P('req', None, 'tp'), may hold values from -0.125 to 0.125
- w_up: bfloat16 [64, 2048, 1408], P('req', None, 'tp'), may hold values from -0.125 to 0.125
- w_down: bfloat16 [64, 1408, 2048], P('req', 'tp'), may hold values from -0.15625 to 0.15625
- latent_cache: bfloat16 [2048, 64, 576], P('req'), may hold values from -3000 to 3000
- page_table: int32 [256, 8], P('req'), may hold values from 0 to 7, as said below
- cache_len: int32 [256], P('req'), may hold values from 1 to 512, 65536 in all
- parents: int32 [256, 3, 8], P('req'), may hold values from 0 to 7
- routes: int32 [8192, 6], P('req'), may hold values from 0 to 63, all different within a row; in each aligned block of 128 rows (0 to 127, 128 to 255, ...) at most 24 rows name the same one
- route_weights: float32 [8192, 6], P('req'), may hold values from 0.1 to 1
Outputs:
- layer_out: bfloat16 [8192, 2048], P('req', 'tp')
Inputs may be any that keep to these rules, and one draw needn't show every extreme that they name: `page_table`: each request's row lists the 8 pages of that request's block of the pool, each once. `routes`: each row names 6 different experts; in the rows of one index of req no expert is named more than 24 times, a bound that some block reaches.
All inputs are finite; a program needn't handle non-finite values. No bound on the sum of `cache_len` on one device may be relied on, other than what follows from the above.
Results may differ from a plain program's by a relative error of at most 0.015.
The roundings to bfloat16 on the way count: a program that leaves them out, or rounds other values in their place, can miss the bound.
Values may be sent and summed in bfloat16 or wider, within the bound.
No kernel may reach another device: no remote copies, remote signals or barrier semaphores. Data moves between devices by JAX's collectives and lax.ppermute only.
A program may use at most 128 MiB of HBM per device.

v0:
```python
import jax
import jax.numpy as jnp
from jax import lax
from jax.sharding import PartitionSpec as P

D = 2048
NOPE = 128
ROPE = 64
VDIM = 128
LATENT = 512
TOPK = 6
EXP_DEV = 1
BEAMS = 8
STEPS = 4
PAGE = 64
PAGES = 8
eps = 1e-06
rope_base = 50000.0


def rms_scale(values):
    return lax.rsqrt(jnp.mean(values * values, axis=-1, keepdims=True) + eps)


def rotate(values, cos_val, sin_val):
    half_rope = values.shape[-1] // 2
    first = values[..., :half_rope]
    second = values[..., half_rope:]
    return jnp.concatenate(
        [first * cos_val - second * sin_val, second * cos_val + first * sin_val], axis=-1
    )


def expert_math(arrived, gate_w, up_w, down_w):
    gate_val = jnp.einsum("nesd,edf->nesf", arrived, gate_w, preferred_element_type=jnp.float32)
    up_val = jnp.einsum("nesd,edf->nesf", arrived, up_w, preferred_element_type=jnp.float32)
    active = (jax.nn.silu(gate_val) * up_val).astype(jnp.bfloat16)
    return jnp.einsum("nesf,efd->nesd", active, down_w, preferred_element_type=jnp.float32)


def send_home(shares):
    return lax.all_to_all(shares, "req", split_axis=0, concat_axis=0, tiled=True)


def local(
    hidden_in,
    attn_gain,
    w_query,
    w_latent,
    kv_gain,
    w_key_up,
    w_value_up,
    w_out,
    moe_gain,
    w_gate,
    w_up,
    w_down,
    latent_cache,
    page_table,
    cache_len,
    parents,
    routes,
    route_weights,
):
    highest = lax.Precision.HIGHEST
    row_count = hidden_in.shape[0]
    req_local = cache_len.shape[0]
    heads_local = w_value_up.shape[1] // VDIM
    tp_count = lax.axis_size("tp")
    req_count = lax.axis_size("req")
    col_share = D // tp_count
    max_len = PAGES * PAGE
    hidden_f = hidden_in.astype(jnp.float32)
    normed = (hidden_f * rms_scale(hidden_f) * attn_gain).astype(jnp.bfloat16)
    positions = (
        cache_len.astype(jnp.float32)[:, None, None]
        + jnp.arange(STEPS, dtype=jnp.float32)[None, :, None]
        + jnp.zeros((1, 1, BEAMS), jnp.float32)
    ).reshape(row_count)
    frequency = rope_base ** (-2.0 * jnp.arange(ROPE // 2, dtype=jnp.float32) / ROPE)
    angles = positions[:, None] * frequency[None, :]
    cos_val = jnp.cos(angles)
    sin_val = jnp.sin(angles)
    queries = jnp.dot(normed, w_query, preferred_element_type=jnp.float32).reshape(
        row_count, heads_local, NOPE + ROPE
    )
    q_nope = queries[:, :, :NOPE].astype(jnp.bfloat16)
    q_rope = rotate(queries[:, :, NOPE:], cos_val[:, None, :], sin_val[:, None, :]).astype(
        jnp.bfloat16
    )
    kv_part = jnp.dot(normed, w_latent, preferred_element_type=jnp.float32)
    kv_all = lax.all_gather(kv_part, "tp", axis=1, tiled=True)
    new_lat = kv_all[:, :LATENT] * rms_scale(kv_all[:, :LATENT]) * kv_gain
    new_rope = rotate(kv_all[:, LATENT:], cos_val, sin_val)
    new_keys = jnp.concatenate([new_lat, new_rope], axis=1).astype(jnp.bfloat16)
    key_up = w_key_up.reshape(LATENT, heads_local, NOPE)
    q_lat = jnp.einsum("nhc,lhc->nhl", q_nope, key_up, preferred_element_type=jnp.float32).astype(
        jnp.bfloat16
    )
    query_key = jnp.concatenate([q_lat, q_rope], axis=2)
    pool_index = (jnp.arange(req_local, dtype=jnp.int32) * PAGES)[:, None] + page_table
    cache_keys = jnp.take(latent_cache, pool_index.reshape(-1), axis=0).reshape(
        req_local, max_len, LATENT + ROPE
    )
    live_mask = jnp.arange(max_len, dtype=jnp.int32)[None, :] < cache_len[:, None]
    score_scale = (NOPE + ROPE) ** (-0.5)
    grouped = query_key.reshape(req_local, STEPS * BEAMS * heads_local, LATENT + ROPE)
    s_cache = (
        jnp.einsum("rqd,rld->rql", grouped, cache_keys, preferred_element_type=jnp.float32)
        * score_scale
    )
    s_cache = jnp.where(live_mask[:, None, :], s_cache, -jnp.inf).reshape(
        req_local, STEPS, BEAMS, heads_local, max_len
    )
    fresh = new_keys.reshape(req_local, STEPS, BEAMS, LATENT + ROPE).astype(jnp.float32)
    parent_hot = (parents[..., None] == jnp.arange(BEAMS, dtype=jnp.int32)).astype(jnp.float32)
    identity = jnp.broadcast_to(jnp.eye(BEAMS, dtype=jnp.float32), (req_local, BEAMS, BEAMS))
    tail_rows = []
    for step_index in range(STEPS):
        lineage = identity
        pieces = [None] * STEPS
        for earlier in range(step_index, -1, -1):
            pieces[earlier] = jnp.einsum(
                "rba,rad->rbd", lineage, fresh[:, earlier], precision=highest
            )
            if earlier > 0:
                lineage = jnp.einsum(
                    "rba,rac->rbc", lineage, parent_hot[:, earlier - 1], precision=highest
                )
        for later in range(step_index + 1, STEPS):
            pieces[later] = jnp.zeros_like(pieces[0])
        tail_rows.append(jnp.stack(pieces, axis=2))
    tail_keys = jnp.stack(tail_rows, axis=1).astype(jnp.bfloat16)
    queries_tail = query_key.reshape(req_local, STEPS, BEAMS, heads_local, LATENT + ROPE)
    s_tail = (
        jnp.einsum(
            "rsbhd,rsbjd->rsbhj", queries_tail, tail_keys, preferred_element_type=jnp.float32
        )
        * score_scale
    )
    causal = jnp.arange(STEPS)[None, :] <= jnp.arange(STEPS)[:, None]
    s_tail = jnp.where(causal[None, :, None, None, :], s_tail, -jnp.inf)
    top_score = jnp.maximum(jnp.max(s_cache, axis=-1), jnp.max(s_tail, axis=-1))
    e_cache = jnp.exp(s_cache - top_score[..., None])
    e_tail = jnp.exp(s_tail - top_score[..., None])
    total = jnp.sum(e_cache, axis=-1) + jnp.sum(e_tail, axis=-1)
    p_cache = (e_cache / total[..., None]).astype(jnp.bfloat16)
    p_tail = (e_tail / total[..., None]).astype(jnp.bfloat16)
    context = jnp.einsum(
        "rsbhl,rld->rsbhd", p_cache, cache_keys[..., :LATENT], preferred_element_type=jnp.float32
    )
    context = context + jnp.einsum(
        "rsbhj,rsbjd->rsbhd", p_tail, tail_keys[..., :LATENT], preferred_element_type=jnp.float32
    )
    context = context.astype(jnp.bfloat16).reshape(row_count, heads_local, LATENT)
    value_up = w_value_up.reshape(LATENT, heads_local, VDIM)
    head_out = (
        jnp.einsum("nhl,lhv->nhv", context, value_up, preferred_element_type=jnp.float32)
        .astype(jnp.bfloat16)
        .reshape(row_count, heads_local * VDIM)
    )
    attn_part = jnp.dot(head_out, w_out, preferred_element_type=jnp.float32)
    expert_count = EXP_DEV * req_count
    capacity = min(row_count, 2 * row_count * TOPK // expert_count)
    slot_count = expert_count * capacity
    picks = routes.reshape(-1)
    pick_hot = (picks[:, None] == jnp.arange(expert_count, dtype=jnp.int32)[None, :]).astype(
        jnp.int32
    )
    before = jnp.cumsum(pick_hot, axis=0) - pick_hot
    ranks = jnp.sum(before * pick_hot, axis=1)
    slot_of = picks * capacity + ranks
    slot_hot = (slot_of[:, None] == jnp.arange(slot_count, dtype=jnp.int32)[None, :]).reshape(
        row_count, TOPK, slot_count
    )
    gather_rows = jnp.sum(slot_hot.astype(jnp.int32), axis=1).astype(jnp.bfloat16)
    weight_rows = jnp.sum(jnp.where(slot_hot, route_weights[:, :, None], 0.0), axis=1)
    tp_index = lax.axis_index("tp")
    col_start = tp_index * col_share
    attn_full = lax.psum(attn_part, "tp")
    resid_full = hidden_f + attn_full
    moe_in = (resid_full * rms_scale(resid_full) * moe_gain).astype(jnp.bfloat16)
    placed = jnp.dot(gather_rows.T, moe_in, preferred_element_type=jnp.float32).astype(jnp.bfloat16)
    partial_out = expert_math(
        lax.all_to_all(
            placed.reshape(req_count, EXP_DEV, capacity, moe_in.shape[1]),
            "req",
            split_axis=0,
            concat_axis=0,
            tiled=True,
        ),
        w_gate,
        w_up,
        w_down,
    )
    shares = lax.psum_scatter(partial_out, "tp", scatter_dimension=3, tiled=True)
    returned = send_home(shares.astype(jnp.bfloat16))
    resid_cols = lax.dynamic_slice_in_dim(resid_full, col_start, col_share, 1)
    combined = jnp.dot(
        weight_rows, returned.reshape(slot_count, col_share).astype(jnp.float32), precision=highest
    )
    return (resid_cols + combined).astype(jnp.bfloat16)


def solution(mesh):
    in_specs = (
        P("req", None),
        P(),
        P(None, "tp"),
        P(None, "tp"),
        P(),
        P(None, "tp"),
        P(None, "tp"),
        P("tp", None),
        P(),
        P("req", None, "tp"),
        P("req", None, "tp"),
        P("req", "tp", None),
        P("req", None, None),
        P("req", None),
        P("req"),
        P("req", None, None),
        P("req", None),
        P("req", None),
    )
    out_specs = P("req", "tp")
    return jax.shard_map(local, mesh=mesh, in_specs=in_specs, out_specs=out_specs, check_vma=False)
```

profile of v0, /device:TPU:1, one launch (start us, length us, event | category | flops | bytes accessed | tf_op | source)
XLA Modules:
  0.0 477.5 jit_solution(17207747423116017685)
XLA Ops:
  7.1 0.8 iota_compare_fusion.3
  8.2 1.2 fusion.40
  9.5 1.6 fusion.63
  11.1 11.2 %all_gather.3 = f32[128,576]{0,1:T(8,128)S(1)} all-gather(f32[128,144]{0,1:T(8,128)S(1)} %fusion.63), channel_id=1, replica_groups=mesh['req'=64,'tp'=4] {'tp'}, dimensions={1}, use_global_device_ids=true | all-gather | bytes 368640 | tf_op jit(solution)/shard_map/all_gather | solution.py:92
  22.4 0.8 multiply_convert_fusion.2
  23.2 1.6 copy.150
  25.1 0.8 multiply_cosine_fusion
  26.4 1.0 pad_maximum_fusion.2
  27.4 0.8 fusion.37
  28.3 0.8 fusion.34
  29.1 0.8 fusion.38
  30.1 0.8 fusion.30
  30.9 0.8 fusion.32
  31.6 0.8 fusion.35
  32.4 0.8 fusion.39
  35.0 0.8 fusion.36
  35.8 0.8 fusion.33
  36.6 0.8 fusion.31
  38.8 2.4 fusion.65
  41.5 1.4 fusion.22
  42.9 0.9 subtract_convert_fusion
  44.5 1.2 reshape.300
  46.0 4.1 gather_fusion
  50.1 2.1 bitcast_select_fusion
  52.3 2.0 fusion.86
  54.5 0.9 maximum_bitcast_fusion
  55.6 3.1 fusion.87
  59.0 1.2 fusion.58
  60.2 2.6 reshape.302
  62.8 1.5 exponential_reduce_fusion
  64.6 1.7 fusion.51
  66.3 0.9 fusion.21
  67.3 1.4 copy.179
  69.1 1.5 fusion.88
  71.2 1.8 reduce-window.6
  74.4 50.8 %all-reduce.2.cloned.1.call-done = f32[128,2048]{1,0:T(8,128)} async-done(((f32[128,2048]{1,0:T(8,128)}), f32[128,2048]{1,0:T(8,128)}) %all-reduce.2.cloned.1.call-update) | async-done | bytes 1048592 | tf_op jit(solution)/shard_map/psum | solution.py:180
  125.1 1.4 multiply_reduce_fusion
  126.6 1.9 convolution_convert_fusion
  128.5 151.6 %all_to_all.10 = bf16[64,1,24,2048]{3,2,1,0:T(8,128)(2,1)S(1)} all-to-all(bf16[64,1,24,2048]{3,2,1,0:T(8,128)(2,1)S(1)} %bitcast.216), channel_id=1, replica_groups=mesh['req'=64,'tp'=4] {'req'}, dimensions={0} | all-to-all | bytes 12582912 | tf_op jit(solution)/shard_map/all_to_all | solution.py:185
  280.1 2.6 copy-done.2
  282.6 5.0 %fusion.2 = f32[64,24,352]{2,1,0:T(8,128)} fusion(bf16[64,1,24,2048]{3,2,1,0:T(8,128)(2,1)S(1)} %all_to_all.10, bf16[1,2048,352]{1,2,0:T(8,128)(2,1)S(1)} %copy-done.25), kind=kOutput, calls=%fused_computation.4 | convolution fusion | flops 2214592512 | bytes 9895936 | tf_op jit(solution)/shard_map/nesd,edf->nesf/dot_general | solution.py:35
  287.7 12.3 %convolution_bitcast_fusion = f32[64,1,24,2048]{3,2,0,1:T(8,128)} fusion(bf16[1,352,2048]{2,1,0:T(8,128)(2,1)S(1)} %copy-done.26, bf16[1,2048,352]{1,2,0:T(8,128)(2,1)} %param.28, bf16[64,1,24,2048]{3,2,1,0:T(8,128)(2,1)} %copy-done.2, f32[64,24,352]{2,1,0:T(8,128)} %fusion.2), kind=kOutput, calls=%fused_computation.6 | convolution fusion | flops 4432429056 | bytes 23920640 | tf_op jit(solution)/shard_map/nesf,efd->nesd/dot_general | solution.py:38
  300.0 114.4 %reduce-scatter.2.cloned.1.call-done = f32[64,1,24,512]{3,2,0,1:T(8,128)} async-done(((f32[64,1,24,2048]{3,2,0,1:T(8,128)}), f32[64,1,24,512]{3,2,0,1:T(8,128)}) %reduce-scatter.2.cloned.1.call-update) | async-done | bytes 3145744 | tf_op jit(solution)/shard_map/reduce_scatter | solution.py:196
  414.4 3.2 convert_bitcast_fusion
  417.7 10.9 %all-to-all-start.1 = ((bf16[64,1,24,512]{3,2,1,0:T(8,128)(2,1)}), bf16[64,1,24,512]{3,2,1,0:T(8,128)(2,1)}, u32[]{:S(2)}, u32[]{:S(2)}) async-start(bf16[64,1,24,512]{3,2,1,0:T(8,128)(2,1)} %convert_bitcast_fusion), calls=%async_computation.2 | async-start | bytes 3145728 | tf_op jit(solution)/shard_map/all_to_all | solution.py:42
  428.6 1.5 select_reduce_fusion
  430.2 37.4 %all-to-all-done.1 = bf16[64,1,24,512]{3,2,1,0:T(8,128)(2,1)} async-done(((bf16[64,1,24,512]{3,2,1,0:T(8,128)(2,1)}), bf16[64,1,24,512]{3,2,1,0:T(8,128)(2,1)}, u32[]{:S(2)}, u32[]{:S(2)}) %all-to-all-start.1) | async-done | bytes 1572896 | tf_op jit(solution)/shard_map/all_to_all | solution.py:42
  467.6 3.1 fusion.29
  (120 shorter events, 9.7 us)
Async XLA Ops:
  6.5 32.2 %copy-start = (bf16[2048,768]{1,0:T(8,128)(2,1)S(1)}, bf16[2048,768]{1,0:T(8,128)(2,1)}, u32[]{:S(2)}) copy-start(bf16[2048,768]{1,0:T(8,128)(2,1)} %param.20) | copy-start | bytes 9437188
  6.5 15.8 %copy-start.21 = (f32[512]{0:T(512)S(1)}, f32[512]{0:T(512)}, u32[]{:S(2)}) copy-start(f32[512]{0:T(512)} %param.22) | copy-start | bytes 6148
  6.5 18.3 %copy-start.23 = (s32[4]{0:T(128)S(1)}, s32[4]{0:T(128)}, u32[]{:S(2)}) copy-start(s32[4]{0:T(128)} %param.32) | copy-start | bytes 52
  6.5 118.6 %all-reduce.2.cloned.1.call-start = ((), (), s32[]{:S(2)}) async-start(), calls=%async_computation.3 | async-start | bytes 2097152 | tf_op jit(solution)/shard_map/psum | solution.py:180
  9.5 29.3 %copy-start.18 = (f32[2048]{0:T(1024)S(1)}, f32[2048]{0:T(1024)}, u32[]{:S(2)}) copy-start(f32[2048]{0:T(1024)} %param.19) | copy-start | bytes 24580
  42.9 2.8 copy-start.22
  42.9 2.8 copy-start.24
  44.0 6.1 %copy-start.6 = (bf16[128,4,576]{2,0,1:T(8,128)(2,1)}, bf16[128,4,576]{2,0,1:T(8,128)(2,1)S(1)}, u32[]{:S(2)}) copy-start(bf16[128,4,576]{2,0,1:T(8,128)(2,1)S(1)} %pad_maximum_fusion) | copy-start | bytes 1769476
  50.1 2.1 copy-start.5
  52.2 2.3 copy-start.10
  52.2 2.3 copy-start.11
  52.2 2.3 copy-start.12
  52.2 2.3 copy-start.13
  52.2 2.3 copy-start.14
  52.2 2.3 copy-start.15
  52.3 2.3 copy-start.16
  54.3 1.4 copy-start.27
  55.6 3.1 copy-start.7
  58.7 5.9 %slice-start = ((bf16[4,4,8,4,576]{4,2,0,3,1:T(8,128)(2,1)}), bf16[4,4,8,4,512]{4,2,0,3,1:T(8,128)(2,1)S(1)}, s32[]{:S(2)}) async-start(bf16[4,4,8,4,576]{4,2,0,3,1:T(8,128)(2,1)} %copy-done.7), calls=%async_computation.5 | async-start | bytes 1048576 | tf_op jit(solution)/shard_map/slice | solution.py:153
  64.6 1.7 copy-start.9
  67.3 1.8 copy-start.8
  69.0 1.8 copy-start.17
  70.5 54.6 %copy-start.4 = (bf16[128,2048]{1,0:T(8,128)(2,1)S(1)}, bf16[128,2048]{1,0:T(8,128)(2,1)}, u32[]{:S(2)}) copy-start(bf16[128,2048]{1,0:T(8,128)(2,1)} %param.18) | copy-start | bytes 1572868
  70.6 343.9 %reduce-scatter.2.cloned.1.call-start = ((), (), s32[]{:S(2)}) async-start(), calls=%async_computation.4 | async-start | bytes 15728640 | tf_op jit(solution)/shard_map/reduce_scatter | solution.py:196
  70.9 55.7 %copy-start.19 = (f32[2048]{0:T(1024)S(1)}, f32[2048]{0:T(1024)}, u32[]{:S(2)}) copy-start(f32[2048]{0:T(1024)} %param.26) | copy-start | bytes 24580
  126.6 1.9 copy-start.3
  128.5 154.2 %copy-start.25 = (bf16[1,2048,352]{1,2,0:T(8,128)(2,1)S(1)}, bf16[1,2048,352]{1,2,0:T(8,128)(2,1)}, u32[]{:S(2)}) copy-start(bf16[1,2048,352]{1,2,0:T(8,128)(2,1)} %param.27) | copy-start | bytes 4325380
  280.1 2.6 copy-start.2
  282.6 5.0 %copy-start.26 = (bf16[1,352,2048]{2,1,0:T(8,128)(2,1)S(1)}, bf16[1,352,2048]{2,1,0:T(8,128)(2,1)}, u32[]{:S(2)}) copy-start(bf16[1,352,2048]{2,1,0:T(8,128)(2,1)} %param.29) | copy-start | bytes 4325380
  417.7 11.0 %copy-start.20 = (f32[128,6]{0,1:T(8,128)S(1)}, f32[128,6]{0,1:T(8,128)}, u32[]{:S(2)}) copy-start(f32[128,6]{0,1:T(8,128)} %param.35) | copy-start | bytes 9220
  417.7 49.9 %all-to-all-start.1 = ((bf16[64,1,24,512]{3,2,1,0:T(8,128)(2,1)}), bf16[64,1,24,512]{3,2,1,0:T(8,128)(2,1)}, u32[]{:S(2)}, u32[]{:S(2)}) async-start(bf16[64,1,24,512]{3,2,1,0:T(8,128)(2,1)} %convert_bitcast_fusion), calls=%async_computation.2 | async-start | bytes 3145728 | tf_op jit(solution)/shard_map/all_to_all | solution.py:42
  428.6 42.1 %copy-start.1 = (bf16[2048,768]{1,0:T(8,128)(2,1)S(1)}, bf16[2048,768]{1,0:T(8,128)(2,1)}, u32[]{:S(2)}) copy-start(bf16[2048,768]{1,0:T(8,128)(2,1)} %param.20) | copy-start | bytes 9437188
Sparse Core Ops, SparseCore 0:
  70.7 54.3 all-reduce.1
  300.1 114.2 reduce-scatter.1
where the time goes:
time: 478 us
  waiting for transfers between devices  203 us (42%)
  blocking collectives  163 us (34%)
  matrix products  45.9 us (10%)
  other arithmetic  23 us (5%)
  local copies, waits for them, and re-layouts  18.1 us (4%)
  between operations  14 us (3%)
  starting transfers between devices  11.2 us (2%)
    all_to_all x1, blocking collectives, local(): lax.all_to_all(placed.reshape(req_count, EXP_DEV, capacity, moe_in.shape[...  152 us
    reduce_scatter x1, waiting for transfers between devices, local(): lax.psum_scatter(partial_out, 'tp', scatter_dimension=3, tiled=True)  114 us
    psum x1, waiting for transfers between devices, local(): attn_full = lax.psum(attn_part, 'tp')  50.8 us
    all_to_all x1, waiting for transfers between devices, send_home(): lax.all_to_all(shares, 'req', split_axis=0, concat_axis=0, tiled=True)  37.4 us
    dot_general x1, matrix products, expert_math(): jnp.einsum('nesf,efd->nesd', active, down_w, preferred_element_type=jnp.f...  12.3 us
    all_gather x1, blocking collectives, local(): kv_all = lax.all_gather(kv_part, 'tp', axis=1, tiled=True)  11.2 us
    all_to_all x1, starting transfers between devices, send_home(): lax.all_to_all(shares, 'req', split_axis=0, concat_axis=0, tiled=True)  10.9 us
  transfers between devices with their start and end apart: 3, of which 3 were waited for; matrix products, arithmetic and copies ran while one was open for 1% of the time, Pallas kernels for 0%

commit v1 on v0

--- a/solution.py
+++ b/solution.py
@@ -89,7 +89,12 @@
         jnp.bfloat16
     )
     kv_part = jnp.dot(normed, w_latent, preferred_element_type=jnp.float32)
-    kv_all = lax.all_gather(kv_part, "tp", axis=1, tiled=True)
+    ring = [kv_part]
+    for hop in range(3):
+        ring.append(lax.ppermute(ring[-1], "tp", [(dev, (dev + 1) % 4) for dev in range(4)]))
+    kv_all = jnp.roll(
+        jnp.concatenate(ring[::-1], axis=1), (lax.axis_index("tp") + 1) * ring[0].shape[1], axis=1
+    )
     new_lat = kv_all[:, :LATENT] * rms_scale(kv_all[:, :LATENT]) * kv_gain
     new_rope = rotate(kv_all[:, LATENT:], cos_val, sin_val)
     new_keys = jnp.concatenate([new_lat, new_rope], axis=1).astype(jnp.bfloat16)

time: 478 us -> 481 us (level)
  blocking collectives: 163 us -> 152 us
  local copies, waits for them, and re-layouts: 18.1 us -> 24.1 us
  waiting for transfers between devices: 203 us -> 209 us
    all_gather x1 -> x0, blocking collectives: 11.2 us -> none  [local(): kv_all = lax.all_gather(kv_part, 'tp', axis=1, tiled=True)]
    ppermute x0 -> x3, waiting for transfers between devices: none -> 7.6 us  [local(): lax.ppermute(ring[-1], 'tp', [(dev, (dev + 1) % 4) for dev in range(4)])]
  transfers between devices with their start and end apart: 3 -> 6, of which waited for: 3 -> 5; matrix products, arithmetic and copies ran while one was open for 1% -> 5% of each run, Pallas kernels for 0% -> 0%
where the time goes in v1:
time: 481 us; the launch traced here: 480 us
  waiting for transfers between devices  209 us (43%)
  blocking collectives  152 us (32%)
  matrix products  45.1 us (9%)
  local copies, waits for them, and re-layouts  24.1 us (5%)
  other arithmetic  22.3 us (5%)
  starting transfers between devices  14.3 us (3%)
  between operations  13.9 us (3%)
    all_to_all x1, blocking collectives, local(): lax.all_to_all(placed.reshape(req_count, EXP_DEV, capacity, moe_in.shape[...  152 us
    reduce_scatter x1, waiting for transfers between devices, local(): lax.psum_scatter(partial_out, 'tp', scatter_dimension=3, tiled=True)  114 us
    psum x1, waiting for transfers between devices, local(): attn_full = lax.psum(attn_part, 'tp')  49.1 us
    all_to_all x1, waiting for transfers between devices, send_home(): lax.all_to_all(shares, 'req', split_axis=0, concat_axis=0, tiled=True)  37.4 us
    dot_general x1, matrix products, expert_math(): jnp.einsum('nesf,efd->nesd', active, down_w, preferred_element_type=jnp.f...  12.3 us
    all_to_all x1, starting transfers between devices, send_home(): lax.all_to_all(shares, 'req', split_axis=0, concat_axis=0, tiled=True)  10.9 us
  transfers between devices with their start and end apart: 6, of which 5 were waited for; matrix products, arithmetic and copies ran while one was open for 5% of the time, Pallas kernels for 0%

profile of v1, /device:TPU:1, one launch (start us, length us, event | category | flops | bytes accessed | tf_op | source)
XLA Modules:
  0.0 480.0 jit_solution(17984528509107629074)
XLA Ops:
  6.5 1.4 fusion.40
  7.9 1.6 fusion.63
  9.6 2.1 collective-permute-start
  14.9 2.1 fusion.65
  19.4 4.1 gather_fusion
  23.5 2.0 bitcast_select_fusion
  25.7 0.8 copy.180
  26.6 0.8 copy.181
  27.4 2.1 copy.179
  29.5 1.2 collective-permute-start.1
  30.8 3.2 collective-permute-done.1
  34.0 4.4 collective-permute-done.2
  39.5 1.6 multiply_cosine_fusion
  42.0 0.8 pad_maximum_fusion.2
  43.0 0.9 fusion.34
  43.9 0.8 fusion.38
  44.7 0.8 fusion.30
  45.5 0.8 fusion.32
  47.8 0.8 copy.144
  48.6 0.8 copy.146
  49.5 1.1 subtract_convert_fusion
  50.7 0.9 copy-done.6
  51.5 1.3 copy.147
  52.9 2.2 reshape.300
  55.1 3.1 fusion.86
  58.9 1.0 maximum_bitcast_fusion
  60.1 3.1 fusion.87
  63.4 1.2 fusion.58
  64.6 2.6 reshape.302
  67.2 1.5 exponential_reduce_fusion
  69.0 1.7 fusion.51
  70.8 0.9 fusion.21
  72.1 1.2 copy-done.8
  73.3 1.5 fusion.88
  75.3 1.8 reduce-window.6
  78.4 49.1 %all-reduce.2.cloned.1.call-done = f32[128,2048]{1,0:T(8,128)} async-done(((f32[128,2048]{1,0:T(8,128)}), f32[128,2048]{1,0:T(8,128)}) %all-reduce.2.cloned.1.call-update) | async-done | bytes 1048592 | tf_op jit(solution)/shard_map/psum | solution.py:185
  127.6 1.4 multiply_reduce_fusion
  129.0 1.9 convolution_convert_fusion
  130.9 151.6 %all_to_all.10 = bf16[64,1,24,2048]{3,2,1,0:T(8,128)(2,1)S(1)} all-to-all(bf16[64,1,24,2048]{3,2,1,0:T(8,128)(2,1)S(1)} %bitcast.216), channel_id=1, replica_groups=mesh['req'=64,'tp'=4] {'req'}, dimensions={0} | all-to-all | bytes 12582912 | tf_op jit(solution)/shard_map/all_to_all | solution.py:190
  282.5 2.6 copy-done.2
  285.1 5.0 %fusion.2 = f32[64,24,352]{2,1,0:T(8,128)} fusion(bf16[64,1,24,2048]{3,2,1,0:T(8,128)(2,1)S(1)} %all_to_all.10, bf16[1,2048,352]{1,2,0:T(8,128)(2,1)S(1)} %copy-done.23), kind=kOutput, calls=%fused_computation.4 | convolution fusion | flops 2214592512 | bytes 9895936 | tf_op jit(solution)/shard_map/nesd,edf->nesf/dot_general | solution.py:35
  290.1 12.3 %convolution_bitcast_fusion = f32[64,1,24,2048]{3,2,0,1:T(8,128)} fusion(bf16[1,352,2048]{2,1,0:T(8,128)(2,1)S(1)} %copy-done.24, bf16[1,2048,352]{1,2,0:T(8,128)(2,1)} %param.28, bf16[64,1,24,2048]{3,2,1,0:T(8,128)(2,1)} %copy-done.2, f32[64,24,352]{2,1,0:T(8,128)} %fusion.2), kind=kOutput, calls=%fused_computation.6 | convolution fusion | flops 4432429056 | bytes 23920640 | tf_op jit(solution)/shard_map/nesf,efd->nesd/dot_general | solution.py:38
  302.4 114.4 %reduce-scatter.2.cloned.1.call-done = f32[64,1,24,512]{3,2,0,1:T(8,128)} async-done(((f32[64,1,24,2048]{3,2,0,1:T(8,128)}), f32[64,1,24,512]{3,2,0,1:T(8,128)}) %reduce-scatter.2.cloned.1.call-update) | async-done | bytes 3145744 | tf_op jit(solution)/shard_map/reduce_scatter | solution.py:201
  416.9 3.2 convert_bitcast_fusion
  420.1 10.9 %all-to-all-start.1 = ((bf16[64,1,24,512]{3,2,1,0:T(8,128)(2,1)}), bf16[64,1,24,512]{3,2,1,0:T(8,128)(2,1)}, u32[]{:S(2)}, u32[]{:S(2)}) async-start(bf16[64,1,24,512]{3,2,1,0:T(8,128)(2,1)} %convert_bitcast_fusion), calls=%async_computation.2 | async-start | bytes 3145728 | tf_op jit(solution)/shard_map/all_to_all | solution.py:42
  431.1 1.5 select_reduce_fusion
  432.6 37.4 %all-to-all-done.1 = bf16[64,1,24,512]{3,2,1,0:T(8,128)(2,1)} async-done(((bf16[64,1,24,512]{3,2,1,0:T(8,128)(2,1)}), bf16[64,1,24,512]{3,2,1,0:T(8,128)(2,1)}, u32[]{:S(2)}, u32[]{:S(2)}) %all-to-all-start.1) | async-done | bytes 1572896 | tf_op jit(solution)/shard_map/all_to_all | solution.py:42
  470.0 3.1 fusion.29
  (127 shorter events, 13.2 us)
Async XLA Ops:
  6.5 8.4 %copy-start = (bf16[2048,768]{1,0:T(8,128)(2,1)S(1)}, bf16[2048,768]{1,0:T(8,128)(2,1)}, u32[]{:S(2)}) copy-start(bf16[2048,768]{1,0:T(8,128)(2,1)} %param.20) | copy-start | bytes 9437188
  6.5 121.0 %all-reduce.2.cloned.1.call-start = ((), (), s32[]{:S(2)}) async-start(), calls=%async_computation.3 | async-start | bytes 2097152 | tf_op jit(solution)/shard_map/psum | solution.py:185
  6.5 8.4 %copy-start.4 = (bf16[128,2048]{1,0:T(8,128)(2,1)S(1)}, bf16[128,2048]{1,0:T(8,128)(2,1)}, u32[]{:S(2)}) copy-start(bf16[128,2048]{1,0:T(8,128)(2,1)} %param.18) | copy-start | bytes 1572868
  9.6 7.4 %copy-start.12 = (bf16[512,512]{1,0:T(8,128)(2,1)S(1)}, bf16[512,512]{1,0:T(8,128)(2,1)}, u32[]{:S(2)}) copy-start(bf16[512,512]{1,0:T(8,128)(2,1)} %param.23) | copy-start | bytes 1572868
  9.6 19.9 %collective-permute-start = (f32[128,144]{0,1:T(8,128)S(1)}, f32[128,144]{0,1:T(8,128)S(1)}, u32[]{:S(2)}, u32[]{:S(2)}) collective-permute-start(f32[128,144]{0,1:T(8,128)S(1)} %fusion.63), channel_id=1, source_target_pairs={{0,1},{1,2},{2,3},{3,0},{4,5},{5,6},{6,7},{7,4},{8,9},{9,10},{10,1... | collective-permute-start | bytes 221192 | tf_op jit(solution)/shard_map/ppermute | solution.py:94
  14.1 4.5 copy-start.14
  14.9 2.5 copy-start.22
  25.5 13.8 %copy-start.21 = (f32[512]{0:T(512)S(1)}, f32[512]{0:T(512)}, u32[]{:S(2)}) copy-start(f32[512]{0:T(512)} %param.22) | copy-start | bytes 6148
  29.5 4.4 collective-permute-start.1
  33.9 4.4 collective-permute-start.2
  38.5 0.8 copy-start.11
  50.7 0.9 copy-start.6
  55.1 3.2 copy-start.17
  55.1 3.4 copy-start.16
  55.1 3.6 copy-start.15
  55.1 3.8 copy-start.13
  60.0 3.1 copy-start.7
  63.1 5.9 %slice-start = ((bf16[4,4,8,4,576]{4,2,0,3,1:T(8,128)(2,1)}), bf16[4,4,8,4,512]{4,2,0,3,1:T(8,128)(2,1)S(1)}, s32[]{:S(2)}) async-start(bf16[4,4,8,4,576]{4,2,0,3,1:T(8,128)(2,1)} %copy-done.7), calls=%async_computation.5 | async-start | bytes 1048576 | tf_op jit(solution)/shard_map/slice | solution.py:158
  69.0 1.7 copy-start.10
  70.8 1.0 copy-start.9
  71.7 1.6 copy-start.8
  72.1 2.8 copy-start.18
  74.8 52.8 %copy-start.5 = (bf16[128,2048]{1,0:T(8,128)(2,1)S(1)}, bf16[128,2048]{1,0:T(8,128)(2,1)}, u32[]{:S(2)}) copy-start(bf16[128,2048]{1,0:T(8,128)(2,1)} %param.18) | copy-start | bytes 1572868
  74.8 342.1 %reduce-scatter.2.cloned.1.call-start = ((), (), s32[]{:S(2)}) async-start(), calls=%async_computation.4 | async-start | bytes 15728640 | tf_op jit(solution)/shard_map/reduce_scatter | solution.py:201
  75.0 54.0 %copy-start.19 = (f32[2048]{0:T(1024)S(1)}, f32[2048]{0:T(1024)}, u32[]{:S(2)}) copy-start(f32[2048]{0:T(1024)} %param.26) | copy-start | bytes 24580
  129.0 1.9 copy-start.3
  130.9 154.2 %copy-start.23 = (bf16[1,2048,352]{1,2,0:T(8,128)(2,1)S(1)}, bf16[1,2048,352]{1,2,0:T(8,128)(2,1)}, u32[]{:S(2)}) copy-start(bf16[1,2048,352]{1,2,0:T(8,128)(2,1)} %param.27) | copy-start | bytes 4325380
  282.5 2.6 copy-start.2
  285.1 5.0 %copy-start.24 = (bf16[1,352,2048]{2,1,0:T(8,128)(2,1)S(1)}, bf16[1,352,2048]{2,1,0:T(8,128)(2,1)}, u32[]{:S(2)}) copy-start(bf16[1,352,2048]{2,1,0:T(8,128)(2,1)} %param.29) | copy-start | bytes 4325380
  420.1 11.0 %copy-start.20 = (f32[128,6]{0,1:T(8,128)S(1)}, f32[128,6]{0,1:T(8,128)}, u32[]{:S(2)}) copy-start(f32[128,6]{0,1:T(8,128)} %param.35) | copy-start | bytes 9220
  420.1 49.9 %all-to-all-start.1 = ((bf16[64,1,24,512]{3,2,1,0:T(8,128)(2,1)}), bf16[64,1,24,512]{3,2,1,0:T(8,128)(2,1)}, u32[]{:S(2)}, u32[]{:S(2)}) async-start(bf16[64,1,24,512]{3,2,1,0:T(8,128)(2,1)} %convert_bitcast_fusion), calls=%async_computation.2 | async-start | bytes 3145728 | tf_op jit(solution)/shard_map/all_to_all | solution.py:42
  431.1 42.1 %copy-start.1 = (bf16[2048,768]{1,0:T(8,128)(2,1)S(1)}, bf16[2048,768]{1,0:T(8,128)(2,1)}, u32[]{:S(2)}) copy-start(bf16[2048,768]{1,0:T(8,128)(2,1)} %param.20) | copy-start | bytes 9437188
Sparse Core Ops, SparseCore 0:
  74.9 52.5 all-reduce.1
  302.6 114.2 reduce-scatter.1
